TPU v7x, 512 devices: a whole 4x4x16 slice. The times are simulated.
512 devices in a mesh: ta: 32 (over x_hi, z), gz: 8 (over y, x_lo), gy: 2 (over core).
Axes of the slice: x: 4 (x_hi: 2, x_lo: 2; x = x_hi * 2 + x_lo), y: 4, z: 16, core: 2. Of those that a mesh axis runs over, the one named last changes fastest.
Arguments:
- source_field: bfloat16 [32, 16, 4, 2, 256, 128], P('ta', 'gz', 'gy'), may hold values from -6 to 6
- clover: bfloat16 [32, 16, 4, 2, 128, 128], P('ta', 'gz', 'gy'), may hold values from -0.1875 to 0.1875
- forward: bfloat16 [4, 32, 16, 4, 2, 128, 128], P(None, 'ta', 'gz', 'gy'), may hold values from -0.1875 to 0.1875
- backward: bfloat16 [4, 32, 16, 4, 2, 128, 128], P(None, 'ta', 'gz', 'gy'), may hold values from -0.1875 to 0.1875
- restrict_blocks: bfloat16 [32, 16, 4, 2, 128, 128], P('ta', 'gz', 'gy'), may hold values from -0.1875 to 0.1875
Outputs:
- second_image: bfloat16 [32, 16, 4, 2, 256, 128], P('ta', 'gz', 'gy')
- restricted: bfloat16 [32, 16, 256, 128], P('ta')
All inputs are finite; a program needn't handle non-finite values.
Results may differ from a plain program's by a relative error of at most 0.0064.
Values may be sent and summed in bfloat16 or wider, within the bound.
No kernel may reach another device: no remote copies, remote signals or barrier semaphores. Data moves between devices by JAX's collectives and lax.ppermute only.
A program may use at most 64 MiB of HBM per device.

v0:
```python
import jax
import jax.numpy as jnp
from jax import lax
from jax.sharding import PartitionSpec as P


def padded_2(block, sides, width):
    for axis, dim in sides:
        count = lax.axis_size(axis)
        forward = [(i, i + 1) for i in range(count - 1)]
        forward.append((count - 1, 0))
        backward = [(target, source) for source, target in forward]
        low = lax.ppermute(
            lax.slice_in_dim(block, block.shape[dim] - width, None, axis=dim), axis, forward
        )
        high = lax.ppermute(lax.slice_in_dim(block, 0, width, axis=dim), axis, backward)
        block = jnp.concatenate([low, block, high], axis=dim)
    return block


def shifted(block, axis, distance):
    devices = range(lax.axis_size(axis))
    route = [((i - distance) % len(devices), i) for i in devices]
    return lax.ppermute(block, axis, route)


def apply_block(blocks, vector):
    return jnp.einsum("tzyxij,tzyxrj->tzyxri", blocks, vector, preferred_element_type=jnp.float32)


def settle(formed):
    return lax.optimization_barrier(formed).astype(jnp.float32)


def operate_raw(vector, clover, forward, backward, shifted_blocks):
    padded = padded_2(vector, (("ta", 0), ("gz", 1), ("gy", 2)), 1)
    total = apply_block(clover, vector)
    total = total + apply_block(forward[0], padded[2:, 1:-1, 1:-1])
    total = total + apply_block(forward[1], padded[1:-1, 2:, 1:-1])
    total = total + apply_block(forward[2], padded[1:-1, 1:-1, 2:])
    total = total + apply_block(forward[3], jnp.roll(vector, -1, axis=3))
    total = total + settle(
        apply_block(shifted_blocks[0], padded[:-2, 1:-1, 1:-1]).astype(jnp.bfloat16)
    )
    total = total + settle(
        apply_block(shifted_blocks[1], padded[1:-1, :-2, 1:-1]).astype(jnp.bfloat16)
    )
    total = total + settle(
        apply_block(shifted_blocks[2], padded[1:-1, 1:-1, :-2]).astype(jnp.bfloat16)
    )
    formed_x = apply_block(backward[3], vector).astype(jnp.bfloat16)
    total = total + settle(jnp.roll(formed_x, 1, axis=3))
    return total.astype(jnp.bfloat16)


def per_device(source_field, clover, forward, backward, restrict_blocks):
    back_time = backward[0]
    back_zdir = backward[1]
    back_ydir = backward[2]
    shifted_time = jnp.concatenate([shifted(back_time, "ta", 1), back_time[:-1]], axis=0)
    shifted_zdir = jnp.concatenate([shifted(back_zdir[:, -1:], "gz", 1), back_zdir[:, :-1]], axis=1)
    shifted_ydir = jnp.concatenate(
        [shifted(back_ydir[:, :, -1:], "gy", 1), back_ydir[:, :, :-1]], axis=2
    )
    shifted_blocks = (shifted_time, shifted_zdir, shifted_ydir)
    first_image = operate_raw(source_field, clover, forward, backward, shifted_blocks)
    second_image = operate_raw(first_image, clover, forward, backward, shifted_blocks)
    partial_sum = jnp.einsum(
        "tzyxij,tzyxrj->ri", restrict_blocks, second_image, preferred_element_type=jnp.float32
    )
    own_part = partial_sum.astype(jnp.bfloat16).reshape(
        1, 1, partial_sum.shape[0], partial_sum.shape[1]
    )
    restricted = lax.all_gather(own_part, ("gz", "gy"), axis=1, tiled=True)
    return (second_image, restricted)


def solution(mesh):
    return jax.shard_map(
        per_device,
        mesh=mesh,
        in_specs=(
            P("ta", "gz", "gy", None, None, None),
            P("ta", "gz", "gy", None, None, None),
            P(None, "ta", "gz", "gy", None, None, None),
            P(None, "ta", "gz", "gy", None, None, None),
            P("ta", "gz", "gy", None, None, None),
        ),
        out_specs=(P("ta", "gz", "gy", None, None, None), P("ta", None, None, None)),
        check_vma=False,
    )
```

profile of v0, /device:TPU:1, one launch (start us, length us, event | category | flops | bytes accessed | tf_op | source)
XLA Modules:
  0.0 204.1 jit_solution(7602025396160097925)
XLA Ops:
  7.2 4.5 %collective-permute-start.1 = (bf16[1,2,2,2,256,128]{5,4,3,2,1,0:T(8,128)(2,1)}, bf16[1,2,2,2,256,128]{5,4,3,2,1,0:T(8,128)(2,1)S(1)}, u32[]{:S(2)}, u32[]{:S(2)}) collective-permute-start(bf16[1,2,2,2,256,128]{5,4,3,2,1,0:T(8,128)(2,1)} %param.5), channel_id=1, source_target_pairs={{0,16},{16,32},{32,48},{48,64},{64,80},{80,96},{96,112},{112,128},... | collective-permute-start | bytes 1572872 | tf_op jit(solution)/shard_map/ppermute | solution.py:13
  11.7 12.0 %collective-permute-start = (bf16[1,2,2,2,256,128]{5,4,3,2,1,0:T(8,128)(2,1)}, bf16[1,2,2,2,256,128]{5,4,3,2,1,0:T(8,128)(2,1)S(1)}, u32[]{:S(2)}, u32[]{:S(2)}) collective-permute-start(bf16[1,2,2,2,256,128]{5,4,3,2,1,0:T(8,128)(2,1)} %param.5), channel_id=1, source_target_pairs={{16,0},{32,16},{48,32},{64,48},{80,64},{96,80},{112,96},{128,112},... | collective-permute-start | bytes 1572872 | tf_op jit(solution)/shard_map/ppermute | solution.py:16
  23.7 9.9 %collective-permute-done.1 = bf16[1,2,2,2,256,128]{5,4,3,2,1,0:T(8,128)(2,1)S(1)} collective-permute-done((bf16[1,2,2,2,256,128]{5,4,3,2,1,0:T(8,128)(2,1)}, bf16[1,2,2,2,256,128]{5,4,3,2,1,0:T(8,128)(2,1)S(1)}, u32[]{:S(2)}, u32[]{:S(2)}) %collective-permute-start.1) | collective-permute-done | bytes 524320 | tf_op jit(solution)/shard_map/ppermute | solution.py:13
  33.6 1.1 constant_dynamic-update-slice_fusion.1
  35.0 4.8 %collective-permute-start.2 = (bf16[3,1,2,2,256,128]{5,4,3,2,1,0:T(8,128)(2,1)S(1)}, bf16[3,1,2,2,256,128]{5,4,3,2,1,0:T(8,128)(2,1)S(1)}, u32[]{:S(2)}, u32[]{:S(2)}) collective-permute-start(bf16[3,1,2,2,256,128]{5,4,3,2,1,0:T(8,128)(2,1)S(1)} %get-tuple-element.9), channel_id=1, source_target_pairs={{2,0},{4,2},{6,4},{8,6},{10,8},{12,10},{14,12},{0,14},{3,1},{5,3},... | collective-permute-start | bytes 2359304 | tf_op jit(solution)/shard_map/ppermute | solution.py:16
  39.8 1.9 collective-permute-start.3
  41.9 3.6 %collective-permute-start.8 = (bf16[1,2,1,2,128,128]{5,4,3,2,1,0:T(8,128)(2,1)S(1)}, bf16[1,2,1,2,128,128]{5,4,3,2,1,0:T(8,128)(2,1)S(1)}, u32[]{:S(2)}, u32[]{:S(2)}) collective-permute-start(bf16[1,2,1,2,128,128]{5,4,3,2,1,0:T(8,128)(2,1)S(1)} %get-tuple-element.23), channel_id=1, source_target_pairs={{1,0},{0,1},{3,2},{2,3},{5,4},{4,5},{7,6},{6,7},{9,8},{8,9},{11,10... | collective-permute-start | bytes 393224 | tf_op jit(solution)/shard_map/ppermute | solution.py:24
  45.5 2.1 %collective-permute-start.6 = (bf16[1,1,2,2,128,128]{5,4,3,2,1,0:T(8,128)(2,1)S(1)}, bf16[1,1,2,2,128,128]{5,4,3,2,1,0:T(8,128)(2,1)S(1)}, u32[]{:S(2)}, u32[]{:S(2)}) collective-permute-start(bf16[1,1,2,2,128,128]{5,4,3,2,1,0:T(8,128)(2,1)S(1)} %get-tuple-element.21), channel_id=1, source_target_pairs={{14,0},{0,2},{2,4},{4,6},{6,8},{8,10},{10,12},{12,14},{15,1},{1,3}... | collective-permute-start | bytes 393224 | tf_op jit(solution)/shard_map/ppermute | solution.py:24
  47.6 1.9 collective-permute-start.5
  49.5 0.3 fusion.19
  49.8 11.2 %collective-permute-done.2 = bf16[3,1,2,2,256,128]{5,4,3,2,1,0:T(8,128)(2,1)S(1)} collective-permute-done((bf16[3,1,2,2,256,128]{5,4,3,2,1,0:T(8,128)(2,1)S(1)}, bf16[3,1,2,2,256,128]{5,4,3,2,1,0:T(8,128)(2,1)S(1)}, u32[]{:S(2)}, u32[]{:S(2)}) %collective-permute-start.2) | collective-permute-done | bytes 786464 | tf_op jit(solution)/shard_map/ppermute | solution.py:16
  61.0 18.7 %collective-permute-done.3 = bf16[3,1,2,2,256,128]{5,4,3,2,1,0:T(8,128)(2,1)S(1)} collective-permute-done((bf16[3,1,2,2,256,128]{5,4,3,2,1,0:T(8,128)(2,1)S(1)}, bf16[3,1,2,2,256,128]{5,4,3,2,1,0:T(8,128)(2,1)S(1)}, u32[]{:S(2)}, u32[]{:S(2)}) %collective-permute-start.3) | collective-permute-done | bytes 786464 | tf_op jit(solution)/shard_map/ppermute | solution.py:13
  79.7 0.4 pad_maximum_fusion
  80.3 5.5 %collective-permute-start.7 = (bf16[3,4,1,2,256,128]{5,4,3,2,1,0:T(8,128)(2,1)S(1)}, bf16[3,4,1,2,256,128]{5,4,3,2,1,0:T(8,128)(2,1)S(1)}, u32[]{:S(2)}, u32[]{:S(2)}) collective-permute-start(bf16[3,4,1,2,256,128]{5,4,3,2,1,0:T(8,128)(2,1)S(1)} %get-tuple-element.4), channel_id=1, source_target_pairs={{0,1},{1,0},{2,3},{3,2},{4,5},{5,4},{6,7},{7,6},{8,9},{9,8},{10,11... | collective-permute-start | bytes 4718600 | tf_op jit(solution)/shard_map/ppermute | solution.py:13
  85.9 2.1 %collective-permute-start.4 = (bf16[3,4,1,2,256,128]{5,4,3,2,1,0:T(8,128)(2,1)S(1)}, bf16[3,4,1,2,256,128]{5,4,3,2,1,0:T(8,128)(2,1)S(1)}, u32[]{:S(2)}, u32[]{:S(2)}) collective-permute-start(bf16[3,4,1,2,256,128]{5,4,3,2,1,0:T(8,128)(2,1)S(1)} %get-tuple-element.5), channel_id=1, source_target_pairs={{1,0},{0,1},{3,2},{2,3},{5,4},{4,5},{7,6},{6,7},{9,8},{8,9},{11,10... | collective-permute-start | bytes 4718600 | tf_op jit(solution)/shard_map/ppermute | solution.py:16
  88.1 0.3 fusion.51
  88.4 0.3 fusion.65
  88.7 0.3 convolution_add_fusion.3
  89.0 0.3 fusion.16
  89.3 0.3 fusion.17
  89.7 0.3 fusion.18
  90.0 1.3 collective-permute-done.4
  91.3 0.3 fusion.45
  91.6 0.6 fusion.15
  92.3 1.9 collective-permute-start.10
  94.2 7.0 %collective-permute-start.9 = (bf16[1,2,2,2,256,128]{5,4,3,2,1,0:T(8,128)(2,1)S(1)}, bf16[1,2,2,2,256,128]{5,4,3,2,1,0:T(8,128)(2,1)S(1)}, u32[]{:S(2)}, u32[]{:S(2)}) collective-permute-start(bf16[1,2,2,2,256,128]{5,4,3,2,1,0:T(8,128)(2,1)S(1)} %fusion.15), channel_id=1, source_target_pairs={{16,0},{32,16},{48,32},{64,48},{80,64},{96,80},{112,96},{128,112},... | collective-permute-start | bytes 1572872 | tf_op jit(solution)/shard_map/ppermute | solution.py:16
  101.2 9.9 %collective-permute-done.10 = bf16[1,2,2,2,256,128]{5,4,3,2,1,0:T(8,128)(2,1)S(1)} collective-permute-done((bf16[1,2,2,2,256,128]{5,4,3,2,1,0:T(8,128)(2,1)S(1)}, bf16[1,2,2,2,256,128]{5,4,3,2,1,0:T(8,128)(2,1)S(1)}, u32[]{:S(2)}, u32[]{:S(2)}) %collective-permute-start.10) | collective-permute-done | bytes 524320 | tf_op jit(solution)/shard_map/ppermute | solution.py:13
  111.1 0.9 collective-permute-done.9
  112.3 2.2 %collective-permute-start.12 = (bf16[3,1,2,2,256,128]{5,4,3,2,1,0:T(8,128)(2,1)S(1)}, bf16[3,1,2,2,256,128]{5,4,3,2,1,0:T(8,128)(2,1)S(1)}, u32[]{:S(2)}, u32[]{:S(2)}) collective-permute-start(bf16[3,1,2,2,256,128]{5,4,3,2,1,0:T(8,128)(2,1)S(1)} %get-tuple-element.6), channel_id=1, source_target_pairs={{0,2},{2,4},{4,6},{6,8},{8,10},{10,12},{12,14},{14,0},{1,3},{3,5},... | collective-permute-start | bytes 2359304 | tf_op jit(solution)/shard_map/ppermute | solution.py:13
  114.5 5.2 %collective-permute-start.11 = (bf16[3,1,2,2,256,128]{5,4,3,2,1,0:T(8,128)(2,1)S(1)}, bf16[3,1,2,2,256,128]{5,4,3,2,1,0:T(8,128)(2,1)S(1)}, u32[]{:S(2)}, u32[]{:S(2)}) collective-permute-start(bf16[3,1,2,2,256,128]{5,4,3,2,1,0:T(8,128)(2,1)S(1)} %get-tuple-element.7), channel_id=1, source_target_pairs={{2,0},{4,2},{6,4},{8,6},{10,8},{12,10},{14,12},{0,14},{3,1},{5,3},... | collective-permute-start | bytes 2359304 | tf_op jit(solution)/shard_map/ppermute | solution.py:16
  119.7 0.3 fusion.23
  120.0 14.1 %collective-permute-done.12 = bf16[3,1,2,2,256,128]{5,4,3,2,1,0:T(8,128)(2,1)S(1)} collective-permute-done((bf16[3,1,2,2,256,128]{5,4,3,2,1,0:T(8,128)(2,1)S(1)}, bf16[3,1,2,2,256,128]{5,4,3,2,1,0:T(8,128)(2,1)S(1)}, u32[]{:S(2)}, u32[]{:S(2)}) %collective-permute-start.12) | collective-permute-done | bytes 786464 | tf_op jit(solution)/shard_map/ppermute | solution.py:13
  134.1 13.9 %collective-permute-done.11 = bf16[3,1,2,2,256,128]{5,4,3,2,1,0:T(8,128)(2,1)S(1)} collective-permute-done((bf16[3,1,2,2,256,128]{5,4,3,2,1,0:T(8,128)(2,1)S(1)}, bf16[3,1,2,2,256,128]{5,4,3,2,1,0:T(8,128)(2,1)S(1)}, u32[]{:S(2)}, u32[]{:S(2)}) %collective-permute-start.11) | collective-permute-done | bytes 786464 | tf_op jit(solution)/shard_map/ppermute | solution.py:16
  148.0 0.4 pad_maximum_fusion.1
  148.6 3.8 %collective-permute-start.14 = (bf16[3,4,1,2,256,128]{5,4,3,2,1,0:T(8,128)(2,1)S(1)}, bf16[3,4,1,2,256,128]{5,4,3,2,1,0:T(8,128)(2,1)S(1)}, u32[]{:S(2)}, u32[]{:S(2)}) collective-permute-start(bf16[3,4,1,2,256,128]{5,4,3,2,1,0:T(8,128)(2,1)S(1)} %get-tuple-element.2), channel_id=1, source_target_pairs={{0,1},{1,0},{2,3},{3,2},{4,5},{5,4},{6,7},{7,6},{8,9},{9,8},{10,11... | collective-permute-start | bytes 4718600 | tf_op jit(solution)/shard_map/ppermute | solution.py:13
  152.4 1.9 collective-permute-start.13
  154.5 0.3 fusion.54
  154.8 0.3 fusion.60
  155.1 0.3 fusion.20
  155.4 0.3 convolution_add_fusion.1
  155.8 0.3 fusion.21
  156.1 0.3 fusion.22
  156.4 1.4 collective-permute-done.13
  157.7 0.3 fusion.32
  158.1 0.7 fusion.14
  159.0 0.9 fusion.24
  160.0 34.9 %all-gather.3.cloned.1.call-done = bf16[4096,128]{1,0:T(8,128)(2,1)} async-done(((bf16[256,128]{1,0:T(8,128)(2,1)}), bf16[4096,128]{1,0:T(8,128)(2,1)}) %all-gather.3.cloned.1.call-update) | async-done | bytes 1048592 | tf_op jit(solution)/shard_map/all_gather | solution.py:74
  194.9 2.3 %copy.17 = bf16[1,16,256,128]{3,2,1,0:T(8,128)(2,1)} copy(bf16[1,16,256,128]{3,2,1,0:T(8,128)(2,1)} %bitcast.156) | data formatting | bytes 2097152
  (36 shorter events, 1.7 us)
Async XLA Ops:
  7.2 81.2 %copy-start = (bf16[1,2,2,2,128,128]{5,4,3,2,1,0:T(8,128)(2,1)S(1)}, bf16[1,2,2,2,128,128]{5,4,3,2,1,0:T(8,128)(2,1)}, u32[]{:S(2)}) copy-start(bf16[1,2,2,2,128,128]{5,4,3,2,1,0:T(8,128)(2,1)} %param.6) | copy-start | bytes 786436
  7.2 187.7 %all-gather.3.cloned.1.call-start = ((), (), s32[]{:S(2)}) async-start(), calls=%async_computation | async-start | bytes 1114112 | tf_op jit(solution)/shard_map/all_gather | solution.py:74
  7.2 26.4 %collective-permute-start.1 = (bf16[1,2,2,2,256,128]{5,4,3,2,1,0:T(8,128)(2,1)}, bf16[1,2,2,2,256,128]{5,4,3,2,1,0:T(8,128)(2,1)S(1)}, u32[]{:S(2)}, u32[]{:S(2)}) collective-permute-start(bf16[1,2,2,2,256,128]{5,4,3,2,1,0:T(8,128)(2,1)} %param.5), channel_id=1, source_target_pairs={{0,16},{16,32},{32,48},{48,64},{64,80},{80,96},{96,112},{112,128},... | collective-permute-start | bytes 1572872 | tf_op jit(solution)/shard_map/ppermute | solution.py:13
  11.7 23.0 %collective-permute-start = (bf16[1,2,2,2,256,128]{5,4,3,2,1,0:T(8,128)(2,1)}, bf16[1,2,2,2,256,128]{5,4,3,2,1,0:T(8,128)(2,1)S(1)}, u32[]{:S(2)}, u32[]{:S(2)}) collective-permute-start(bf16[1,2,2,2,256,128]{5,4,3,2,1,0:T(8,128)(2,1)} %param.5), channel_id=1, source_target_pairs={{16,0},{32,16},{48,32},{64,48},{80,64},{96,80},{112,96},{128,112},... | collective-permute-start | bytes 1572872 | tf_op jit(solution)/shard_map/ppermute | solution.py:16
  34.8 6.9 %copy-start.3 = (bf16[4,1,2,2,2,128,128]{6,5,4,3,2,1,0:T(8,128)(2,1)S(1)}, bf16[4,1,2,2,2,128,128]{6,5,4,3,2,1,0:T(8,128)(2,1)}, u32[]{:S(2)}) copy-start(bf16[4,1,2,2,2,128,128]{6,5,4,3,2,1,0:T(8,128)(2,1)} %param.8) | copy-start | bytes 3145732
  35.0 14.5 %copy-start.1 = (bf16[1,2,2,2,256,128]{5,4,3,2,1,0:T(8,128)(2,1)S(1)}, bf16[1,2,2,2,256,128]{5,4,3,2,1,0:T(8,128)(2,1)}, u32[]{:S(2)}) copy-start(bf16[1,2,2,2,256,128]{5,4,3,2,1,0:T(8,128)(2,1)} %param.5) | copy-start | bytes 1572868
  35.0 25.9 %collective-permute-start.2 = (bf16[3,1,2,2,256,128]{5,4,3,2,1,0:T(8,128)(2,1)S(1)}, bf16[3,1,2,2,256,128]{5,4,3,2,1,0:T(8,128)(2,1)S(1)}, u32[]{:S(2)}, u32[]{:S(2)}) collective-permute-start(bf16[3,1,2,2,256,128]{5,4,3,2,1,0:T(8,128)(2,1)S(1)} %get-tuple-element.9), channel_id=1, source_target_pairs={{2,0},{4,2},{6,4},{8,6},{10,8},{12,10},{14,12},{0,14},{3,1},{5,3},... | collective-permute-start | bytes 2359304 | tf_op jit(solution)/shard_map/ppermute | solution.py:16
  39.8 39.9 %collective-permute-start.3 = (bf16[3,1,2,2,256,128]{5,4,3,2,1,0:T(8,128)(2,1)S(1)}, bf16[3,1,2,2,256,128]{5,4,3,2,1,0:T(8,128)(2,1)S(1)}, u32[]{:S(2)}, u32[]{:S(2)}) collective-permute-start(bf16[3,1,2,2,256,128]{5,4,3,2,1,0:T(8,128)(2,1)S(1)} %get-tuple-element.8), channel_id=1, source_target_pairs={{0,2},{2,4},{4,6},{6,8},{8,10},{10,12},{12,14},{14,0},{1,3},{3,5},... | collective-permute-start | bytes 2359304 | tf_op jit(solution)/shard_map/ppermute | solution.py:13
  41.9 47.8 %collective-permute-start.8 = (bf16[1,2,1,2,128,128]{5,4,3,2,1,0:T(8,128)(2,1)S(1)}, bf16[1,2,1,2,128,128]{5,4,3,2,1,0:T(8,128)(2,1)S(1)}, u32[]{:S(2)}, u32[]{:S(2)}) collective-permute-start(bf16[1,2,1,2,128,128]{5,4,3,2,1,0:T(8,128)(2,1)S(1)} %get-tuple-element.23), channel_id=1, source_target_pairs={{1,0},{0,1},{3,2},{2,3},{5,4},{4,5},{7,6},{6,7},{9,8},{8,9},{11,10... | collective-permute-start | bytes 393224 | tf_op jit(solution)/shard_map/ppermute | solution.py:24
  45.5 43.9 %collective-permute-start.6 = (bf16[1,1,2,2,128,128]{5,4,3,2,1,0:T(8,128)(2,1)S(1)}, bf16[1,1,2,2,128,128]{5,4,3,2,1,0:T(8,128)(2,1)S(1)}, u32[]{:S(2)}, u32[]{:S(2)}) collective-permute-start(bf16[1,1,2,2,128,128]{5,4,3,2,1,0:T(8,128)(2,1)S(1)} %get-tuple-element.21), channel_id=1, source_target_pairs={{14,0},{0,2},{2,4},{4,6},{6,8},{8,10},{10,12},{12,14},{15,1},{1,3}... | collective-permute-start | bytes 393224 | tf_op jit(solution)/shard_map/ppermute | solution.py:24
  47.6 41.5 %collective-permute-start.5 = (bf16[1,2,2,2,128,128]{5,4,3,2,1,0:T(8,128)(2,1)S(1)}, bf16[1,2,2,2,128,128]{5,4,3,2,1,0:T(8,128)(2,1)S(1)}, u32[]{:S(2)}, u32[]{:S(2)}) collective-permute-start(bf16[1,2,2,2,128,128]{5,4,3,2,1,0:T(8,128)(2,1)S(1)} %get-tuple-element.10), channel_id=1, source_target_pairs={{496,0},{0,16},{16,32},{32,48},{48,64},{64,80},{80,96},{96,112},{1... | collective-permute-start | bytes 786440 | tf_op jit(solution)/shard_map/ppermute | solution.py:24
  80.3 9.3 %collective-permute-start.7 = (bf16[3,4,1,2,256,128]{5,4,3,2,1,0:T(8,128)(2,1)S(1)}, bf16[3,4,1,2,256,128]{5,4,3,2,1,0:T(8,128)(2,1)S(1)}, u32[]{:S(2)}, u32[]{:S(2)}) collective-permute-start(bf16[3,4,1,2,256,128]{5,4,3,2,1,0:T(8,128)(2,1)S(1)} %get-tuple-element.4), channel_id=1, source_target_pairs={{0,1},{1,0},{2,3},{3,2},{4,5},{5,4},{6,7},{7,6},{8,9},{9,8},{10,11... | collective-permute-start | bytes 4718600 | tf_op jit(solution)/shard_map/ppermute | solution.py:13
  85.9 2.2 %copy-start.2 = (bf16[4,1,2,2,2,128,128]{6,5,4,3,2,1,0:T(8,128)(2,1)S(1)}, bf16[4,1,2,2,2,128,128]{6,5,4,3,2,1,0:T(8,128)(2,1)}, u32[]{:S(2)}) copy-start(bf16[4,1,2,2,2,128,128]{6,5,4,3,2,1,0:T(8,128)(2,1)} %param.7) | copy-start | bytes 3145732
  85.9 5.4 %collective-permute-start.4 = (bf16[3,4,1,2,256,128]{5,4,3,2,1,0:T(8,128)(2,1)S(1)}, bf16[3,4,1,2,256,128]{5,4,3,2,1,0:T(8,128)(2,1)S(1)}, u32[]{:S(2)}, u32[]{:S(2)}) collective-permute-start(bf16[3,4,1,2,256,128]{5,4,3,2,1,0:T(8,128)(2,1)S(1)} %get-tuple-element.5), channel_id=1, source_target_pairs={{1,0},{0,1},{3,2},{2,3},{5,4},{4,5},{7,6},{6,7},{9,8},{8,9},{11,10... | collective-permute-start | bytes 4718600 | tf_op jit(solution)/shard_map/ppermute | solution.py:16
  92.3 18.8 %collective-permute-start.10 = (bf16[1,2,2,2,256,128]{5,4,3,2,1,0:T(8,128)(2,1)S(1)}, bf16[1,2,2,2,256,128]{5,4,3,2,1,0:T(8,128)(2,1)S(1)}, u32[]{:S(2)}, u32[]{:S(2)}) collective-permute-start(bf16[1,2,2,2,256,128]{5,4,3,2,1,0:T(8,128)(2,1)S(1)} %fusion.15), channel_id=1, source_target_pairs={{0,16},{16,32},{32,48},{48,64},{64,80},{80,96},{96,112},{112,128},... | collective-permute-start | bytes 1572872 | tf_op jit(solution)/shard_map/ppermute | solution.py:13
  94.2 17.8 %collective-permute-start.9 = (bf16[1,2,2,2,256,128]{5,4,3,2,1,0:T(8,128)(2,1)S(1)}, bf16[1,2,2,2,256,128]{5,4,3,2,1,0:T(8,128)(2,1)S(1)}, u32[]{:S(2)}, u32[]{:S(2)}) collective-permute-start(bf16[1,2,2,2,256,128]{5,4,3,2,1,0:T(8,128)(2,1)S(1)} %fusion.15), channel_id=1, source_target_pairs={{16,0},{32,16},{48,32},{64,48},{80,64},{96,80},{112,96},{128,112},... | collective-permute-start | bytes 1572872 | tf_op jit(solution)/shard_map/ppermute | solution.py:16
  112.3 21.8 %collective-permute-start.12 = (bf16[3,1,2,2,256,128]{5,4,3,2,1,0:T(8,128)(2,1)S(1)}, bf16[3,1,2,2,256,128]{5,4,3,2,1,0:T(8,128)(2,1)S(1)}, u32[]{:S(2)}, u32[]{:S(2)}) collective-permute-start(bf16[3,1,2,2,256,128]{5,4,3,2,1,0:T(8,128)(2,1)S(1)} %get-tuple-element.6), channel_id=1, source_target_pairs={{0,2},{2,4},{4,6},{6,8},{8,10},{10,12},{12,14},{14,0},{1,3},{3,5},... | collective-permute-start | bytes 2359304 | tf_op jit(solution)/shard_map/ppermute | solution.py:13
  114.5 33.4 %collective-permute-start.11 = (bf16[3,1,2,2,256,128]{5,4,3,2,1,0:T(8,128)(2,1)S(1)}, bf16[3,1,2,2,256,128]{5,4,3,2,1,0:T(8,128)(2,1)S(1)}, u32[]{:S(2)}, u32[]{:S(2)}) collective-permute-start(bf16[3,1,2,2,256,128]{5,4,3,2,1,0:T(8,128)(2,1)S(1)} %get-tuple-element.7), channel_id=1, source_target_pairs={{2,0},{4,2},{6,4},{8,6},{10,8},{12,10},{14,12},{0,14},{3,1},{5,3},... | collective-permute-start | bytes 2359304 | tf_op jit(solution)/shard_map/ppermute | solution.py:16
  148.6 7.4 %collective-permute-start.14 = (bf16[3,4,1,2,256,128]{5,4,3,2,1,0:T(8,128)(2,1)S(1)}, bf16[3,4,1,2,256,128]{5,4,3,2,1,0:T(8,128)(2,1)S(1)}, u32[]{:S(2)}, u32[]{:S(2)}) collective-permute-start(bf16[3,4,1,2,256,128]{5,4,3,2,1,0:T(8,128)(2,1)S(1)} %get-tuple-element.2), channel_id=1, source_target_pairs={{0,1},{1,0},{2,3},{3,2},{4,5},{5,4},{6,7},{7,6},{8,9},{9,8},{10,11... | collective-permute-start | bytes 4718600 | tf_op jit(solution)/shard_map/ppermute | solution.py:13
  152.4 5.3 %collective-permute-start.13 = (bf16[3,4,1,2,256,128]{5,4,3,2,1,0:T(8,128)(2,1)S(1)}, bf16[3,4,1,2,256,128]{5,4,3,2,1,0:T(8,128)(2,1)S(1)}, u32[]{:S(2)}, u32[]{:S(2)}) collective-permute-start(bf16[3,4,1,2,256,128]{5,4,3,2,1,0:T(8,128)(2,1)S(1)} %get-tuple-element.3), channel_id=1, source_target_pairs={{1,0},{0,1},{3,2},{2,3},{5,4},{4,5},{7,6},{6,7},{9,8},{8,9},{11,10... | collective-permute-start | bytes 4718600 | tf_op jit(solution)/shard_map/ppermute | solution.py:16
  158.1 1.0 copy-start.5
  159.0 38.2 %copy-start.4 = (bf16[1,2,2,2,256,128]{5,4,3,2,1,0:T(8,128)(2,1)}, bf16[1,2,2,2,256,128]{5,4,3,2,1,0:T(8,128)(2,1)S(1)}, u32[]{:S(2)}) copy-start(bf16[1,2,2,2,256,128]{5,4,3,2,1,0:T(8,128)(2,1)S(1)} %fusion.14) | copy-start | bytes 1572868
Sparse Core Ops, SparseCore 0:
  160.1 34.7 all-gather.2
where the time goes:
time: 205 us; the launch traced here: 204 us
  waiting for transfers between devices  116 us (57%)
  starting transfers between devices  60.4 us (29%)
  between operations  14.5 us (7%)
  matrix products  7.1 us (3%)
  local copies, waits for them, and re-layouts  4.79 us (2%)
    ppermute x6, waiting for transfers between devices, padded_2(): lax.ppermute(lax.slice_in_dim(block, block.shape[dim] - width, None, axis...  52.6 us
    all_gather x1, waiting for transfers between devices, per_device(): restricted = lax.all_gather(own_part, ('gz', 'gy'), axis=1, tiled=True)  34.9 us
    ppermute x6, starting transfers between devices, padded_2(): lax.ppermute(lax.slice_in_dim(block, 0, width, axis=dim), axis, backward)  32.9 us
    ppermute x6, waiting for transfers between devices, padded_2(): lax.ppermute(lax.slice_in_dim(block, 0, width, axis=dim), axis, backward)  28.6 us
    ppermute x6, starting transfers between devices, padded_2(): lax.ppermute(lax.slice_in_dim(block, block.shape[dim] - width, None, axis...  19.9 us
    ppermute x3, starting transfers between devices, shifted(): return lax.ppermute(block, axis, route)  7.56 us
    dot_general x18, matrix products, apply_block(): jnp.einsum('tzyxij,tzyxrj->tzyxri', blocks, vector, preferred_element_typ...  6.17 us
  transfers between devices with their start and end apart: 16, of which 10 were waited for; matrix products, arithmetic and copies ran while one was open for 3% of the time, Pallas kernels for 0%

commit v1 on v0

--- a/solution.py
+++ b/solution.py
@@ -2,6 +2,7 @@
 import jax.numpy as jnp
 from jax import lax
 from jax.sharding import PartitionSpec as P
+from jax.lax import all_to_all, axis_size
 
 
 def padded_2(block, sides, width):
@@ -71,7 +72,12 @@
     own_part = partial_sum.astype(jnp.bfloat16).reshape(
         1, 1, partial_sum.shape[0], partial_sum.shape[1]
     )
-    restricted = lax.all_gather(own_part, ("gz", "gy"), axis=1, tiled=True)
+    queue = []
+    for _ in range(axis_size(("gz", "gy"))):
+        queue.append(own_part)
+    restricted = jnp.concatenate(
+        all_to_all(jnp.stack(queue, axis=0), axis_name=("gz", "gy"), split_axis=0, concat_axis=0), 1
+    )
     return (second_image, restricted)
 
 

time: 205 us -> 175 us (0.85)
  waiting for transfers between devices: 116 us -> 81.2 us
  blocking collectives: 0 us -> 20.5 us
  between operations: 14.5 us -> 1.14 us
    all_gather x1 -> x0, waiting for transfers between devices: 34.9 us -> none  [per_device(): restricted = lax.all_gather(own_part, ('gz', 'gy'), axis=1, tiled=True)]
    all_to_all x0 -> x1, blocking collectives: none -> 20.5 us  [per_device(): all_to_all(jnp.stack(queue, axis=0), axis_name=('gz', 'gy'), split_axis=0...]
  transfers between devices with their start and end apart: 16 -> 15, of which waited for: 10 -> 9; matrix products, arithmetic and copies ran while one was open for 3% -> 4% of each run, Pallas kernels for 0% -> 0%
where the time goes in v1:
time: 175 us; the launch traced here: 174 us
  waiting for transfers between devices  81.2 us (46%)
  starting transfers between devices  60.4 us (35%)
  blocking collectives  20.5 us (12%)
  matrix products  6.46 us (4%)
  local copies, waits for them, and re-layouts  3.66 us (2%)
    ppermute x6, waiting for transfers between devices, padded_2(): lax.ppermute(lax.slice_in_dim(block, block.shape[dim] - width, None, axis...  52.6 us
    ppermute x6, starting transfers between devices, padded_2(): lax.ppermute(lax.slice_in_dim(block, 0, width, axis=dim), axis, backward)  32.9 us
    ppermute x6, waiting for transfers between devices, padded_2(): lax.ppermute(lax.slice_in_dim(block, 0, width, axis=dim), axis, backward)  28.6 us
    all_to_all x1, blocking collectives, per_device(): all_to_all(jnp.stack(queue, axis=0), axis_name=('gz', 'gy'), split_axis=0...  20.5 us
    ppermute x6, starting transfers between devices, padded_2(): lax.ppermute(lax.slice_in_dim(block, block.shape[dim] - width, None, axis...  19.9 us
    ppermute x3, starting transfers between devices, shifted(): return lax.ppermute(block, axis, route)  7.56 us
    dot_general x18, matrix products, apply_block(): jnp.einsum('tzyxij,tzyxrj->tzyxri', blocks, vector, preferred_element_typ...  6.17 us
  transfers between devices with their start and end apart: 15, of which 9 were waited for; matrix products, arithmetic and copies ran while one was open for 4% of the time, Pallas kernels for 0%

profile of v1, /device:TPU:1, one launch (start us, length us, event | category | flops | bytes accessed | tf_op | source)
XLA Modules:
  0.0 174.4 jit_solution(12960062086189796495)
XLA Ops:
  0.6 4.5 %collective-permute-start.1 = (bf16[1,2,2,2,256,128]{5,4,3,2,1,0:T(8,128)(2,1)}, bf16[1,2,2,2,256,128]{5,4,3,2,1,0:T(8,128)(2,1)S(1)}, u32[]{:S(2)}, u32[]{:S(2)}) collective-permute-start(bf16[1,2,2,2,256,128]{5,4,3,2,1,0:T(8,128)(2,1)} %param.5), channel_id=1, source_target_pairs={{0,16},{16,32},{32,48},{48,64},{64,80},{80,96},{96,112},{112,128},... | collective-permute-start | bytes 1572872 | tf_op jit(solution)/shard_map/ppermute | solution.py:14
  5.1 12.0 %collective-permute-start = (bf16[1,2,2,2,256,128]{5,4,3,2,1,0:T(8,128)(2,1)}, bf16[1,2,2,2,256,128]{5,4,3,2,1,0:T(8,128)(2,1)S(1)}, u32[]{:S(2)}, u32[]{:S(2)}) collective-permute-start(bf16[1,2,2,2,256,128]{5,4,3,2,1,0:T(8,128)(2,1)} %param.5), channel_id=1, source_target_pairs={{16,0},{32,16},{48,32},{64,48},{80,64},{96,80},{112,96},{128,112},... | collective-permute-start | bytes 1572872 | tf_op jit(solution)/shard_map/ppermute | solution.py:17
  17.1 9.9 %collective-permute-done.1 = bf16[1,2,2,2,256,128]{5,4,3,2,1,0:T(8,128)(2,1)S(1)} collective-permute-done((bf16[1,2,2,2,256,128]{5,4,3,2,1,0:T(8,128)(2,1)}, bf16[1,2,2,2,256,128]{5,4,3,2,1,0:T(8,128)(2,1)S(1)}, u32[]{:S(2)}, u32[]{:S(2)}) %collective-permute-start.1) | collective-permute-done | bytes 524320 | tf_op jit(solution)/shard_map/ppermute | solution.py:14
  27.0 1.1 constant_dynamic-update-slice_fusion.1
  28.4 4.8 %collective-permute-start.2 = (bf16[3,1,2,2,256,128]{5,4,3,2,1,0:T(8,128)(2,1)S(1)}, bf16[3,1,2,2,256,128]{5,4,3,2,1,0:T(8,128)(2,1)S(1)}, u32[]{:S(2)}, u32[]{:S(2)}) collective-permute-start(bf16[3,1,2,2,256,128]{5,4,3,2,1,0:T(8,128)(2,1)S(1)} %get-tuple-element.9), channel_id=1, source_target_pairs={{2,0},{4,2},{6,4},{8,6},{10,8},{12,10},{14,12},{0,14},{3,1},{5,3},... | collective-permute-start | bytes 2359304 | tf_op jit(solution)/shard_map/ppermute | solution.py:17
  33.2 1.9 %collective-permute-start.3 = (bf16[3,1,2,2,256,128]{5,4,3,2,1,0:T(8,128)(2,1)S(1)}, bf16[3,1,2,2,256,128]{5,4,3,2,1,0:T(8,128)(2,1)S(1)}, u32[]{:S(2)}, u32[]{:S(2)}) collective-permute-start(bf16[3,1,2,2,256,128]{5,4,3,2,1,0:T(8,128)(2,1)S(1)} %get-tuple-element.8), channel_id=1, source_target_pairs={{0,2},{2,4},{4,6},{6,8},{8,10},{10,12},{12,14},{14,0},{1,3},{3,5},... | collective-permute-start | bytes 2359304 | tf_op jit(solution)/shard_map/ppermute | solution.py:14
  35.3 3.6 %collective-permute-start.8 = (bf16[1,2,1,2,128,128]{5,4,3,2,1,0:T(8,128)(2,1)S(1)}, bf16[1,2,1,2,128,128]{5,4,3,2,1,0:T(8,128)(2,1)S(1)}, u32[]{:S(2)}, u32[]{:S(2)}) collective-permute-start(bf16[1,2,1,2,128,128]{5,4,3,2,1,0:T(8,128)(2,1)S(1)} %get-tuple-element.23), channel_id=1, source_target_pairs={{1,0},{0,1},{3,2},{2,3},{5,4},{4,5},{7,6},{6,7},{9,8},{8,9},{11,10... | collective-permute-start | bytes 393224 | tf_op jit(solution)/shard_map/ppermute | solution.py:25
  38.9 2.1 %collective-permute-start.6 = (bf16[1,1,2,2,128,128]{5,4,3,2,1,0:T(8,128)(2,1)S(1)}, bf16[1,1,2,2,128,128]{5,4,3,2,1,0:T(8,128)(2,1)S(1)}, u32[]{:S(2)}, u32[]{:S(2)}) collective-permute-start(bf16[1,1,2,2,128,128]{5,4,3,2,1,0:T(8,128)(2,1)S(1)} %get-tuple-element.21), channel_id=1, source_target_pairs={{14,0},{0,2},{2,4},{4,6},{6,8},{8,10},{10,12},{12,14},{15,1},{1,3}... | collective-permute-start | bytes 393224 | tf_op jit(solution)/shard_map/ppermute | solution.py:25
  41.0 1.9 %collective-permute-start.5 = (bf16[1,2,2,2,128,128]{5,4,3,2,1,0:T(8,128)(2,1)S(1)}, bf16[1,2,2,2,128,128]{5,4,3,2,1,0:T(8,128)(2,1)S(1)}, u32[]{:S(2)}, u32[]{:S(2)}) collective-permute-start(bf16[1,2,2,2,128,128]{5,4,3,2,1,0:T(8,128)(2,1)S(1)} %get-tuple-element.10), channel_id=1, source_target_pairs={{496,0},{0,16},{16,32},{32,48},{48,64},{64,80},{80,96},{96,112},{1... | collective-permute-start | bytes 786440 | tf_op jit(solution)/shard_map/ppermute | solution.py:25
  42.9 0.3 fusion.19
  43.2 11.2 %collective-permute-done.2 = bf16[3,1,2,2,256,128]{5,4,3,2,1,0:T(8,128)(2,1)S(1)} collective-permute-done((bf16[3,1,2,2,256,128]{5,4,3,2,1,0:T(8,128)(2,1)S(1)}, bf16[3,1,2,2,256,128]{5,4,3,2,1,0:T(8,128)(2,1)S(1)}, u32[]{:S(2)}, u32[]{:S(2)}) %collective-permute-start.2) | collective-permute-done | bytes 786464 | tf_op jit(solution)/shard_map/ppermute | solution.py:17
  54.4 18.7 %collective-permute-done.3 = bf16[3,1,2,2,256,128]{5,4,3,2,1,0:T(8,128)(2,1)S(1)} collective-permute-done((bf16[3,1,2,2,256,128]{5,4,3,2,1,0:T(8,128)(2,1)S(1)}, bf16[3,1,2,2,256,128]{5,4,3,2,1,0:T(8,128)(2,1)S(1)}, u32[]{:S(2)}, u32[]{:S(2)}) %collective-permute-start.3) | collective-permute-done | bytes 786464 | tf_op jit(solution)/shard_map/ppermute | solution.py:14
  73.1 0.4 pad_maximum_fusion
  73.7 5.5 %collective-permute-start.7 = (bf16[3,4,1,2,256,128]{5,4,3,2,1,0:T(8,128)(2,1)S(1)}, bf16[3,4,1,2,256,128]{5,4,3,2,1,0:T(8,128)(2,1)S(1)}, u32[]{:S(2)}, u32[]{:S(2)}) collective-permute-start(bf16[3,4,1,2,256,128]{5,4,3,2,1,0:T(8,128)(2,1)S(1)} %get-tuple-element.4), channel_id=1, source_target_pairs={{0,1},{1,0},{2,3},{3,2},{4,5},{5,4},{6,7},{7,6},{8,9},{9,8},{10,11... | collective-permute-start | bytes 4718600 | tf_op jit(solution)/shard_map/ppermute | solution.py:14
  79.3 2.1 %collective-permute-start.4 = (bf16[3,4,1,2,256,128]{5,4,3,2,1,0:T(8,128)(2,1)S(1)}, bf16[3,4,1,2,256,128]{5,4,3,2,1,0:T(8,128)(2,1)S(1)}, u32[]{:S(2)}, u32[]{:S(2)}) collective-permute-start(bf16[3,4,1,2,256,128]{5,4,3,2,1,0:T(8,128)(2,1)S(1)} %get-tuple-element.5), channel_id=1, source_target_pairs={{1,0},{0,1},{3,2},{2,3},{5,4},{4,5},{7,6},{6,7},{9,8},{8,9},{11,10... | collective-permute-start | bytes 4718600 | tf_op jit(solution)/shard_map/ppermute | solution.py:17
  81.5 0.3 fusion.51
  81.8 0.3 fusion.65
  82.1 0.3 convolution_add_fusion.3
  82.4 0.3 fusion.16
  82.8 0.3 fusion.17
  83.1 0.3 fusion.18
  83.4 1.3 collective-permute-done.4
  84.7 0.3 fusion.45
  85.0 0.6 fusion.15
  85.7 1.9 %collective-permute-start.10 = (bf16[1,2,2,2,256,128]{5,4,3,2,1,0:T(8,128)(2,1)S(1)}, bf16[1,2,2,2,256,128]{5,4,3,2,1,0:T(8,128)(2,1)S(1)}, u32[]{:S(2)}, u32[]{:S(2)}) collective-permute-start(bf16[1,2,2,2,256,128]{5,4,3,2,1,0:T(8,128)(2,1)S(1)} %fusion.15), channel_id=1, source_target_pairs={{0,16},{16,32},{32,48},{48,64},{64,80},{80,96},{96,112},{112,128},... | collective-permute-start | bytes 1572872 | tf_op jit(solution)/shard_map/ppermute | solution.py:14
  87.6 7.0 %collective-permute-start.9 = (bf16[1,2,2,2,256,128]{5,4,3,2,1,0:T(8,128)(2,1)S(1)}, bf16[1,2,2,2,256,128]{5,4,3,2,1,0:T(8,128)(2,1)S(1)}, u32[]{:S(2)}, u32[]{:S(2)}) collective-permute-start(bf16[1,2,2,2,256,128]{5,4,3,2,1,0:T(8,128)(2,1)S(1)} %fusion.15), channel_id=1, source_target_pairs={{16,0},{32,16},{48,32},{64,48},{80,64},{96,80},{112,96},{128,112},... | collective-permute-start | bytes 1572872 | tf_op jit(solution)/shard_map/ppermute | solution.py:17
  94.6 9.9 %collective-permute-done.10 = bf16[1,2,2,2,256,128]{5,4,3,2,1,0:T(8,128)(2,1)S(1)} collective-permute-done((bf16[1,2,2,2,256,128]{5,4,3,2,1,0:T(8,128)(2,1)S(1)}, bf16[1,2,2,2,256,128]{5,4,3,2,1,0:T(8,128)(2,1)S(1)}, u32[]{:S(2)}, u32[]{:S(2)}) %collective-permute-start.10) | collective-permute-done | bytes 524320 | tf_op jit(solution)/shard_map/ppermute | solution.py:14
  104.5 0.9 collective-permute-done.9
  105.7 2.2 %collective-permute-start.12 = (bf16[3,1,2,2,256,128]{5,4,3,2,1,0:T(8,128)(2,1)S(1)}, bf16[3,1,2,2,256,128]{5,4,3,2,1,0:T(8,128)(2,1)S(1)}, u32[]{:S(2)}, u32[]{:S(2)}) collective-permute-start(bf16[3,1,2,2,256,128]{5,4,3,2,1,0:T(8,128)(2,1)S(1)} %get-tuple-element.6), channel_id=1, source_target_pairs={{0,2},{2,4},{4,6},{6,8},{8,10},{10,12},{12,14},{14,0},{1,3},{3,5},... | collective-permute-start | bytes 2359304 | tf_op jit(solution)/shard_map/ppermute | solution.py:14
  107.9 5.2 %collective-permute-start.11 = (bf16[3,1,2,2,256,128]{5,4,3,2,1,0:T(8,128)(2,1)S(1)}, bf16[3,1,2,2,256,128]{5,4,3,2,1,0:T(8,128)(2,1)S(1)}, u32[]{:S(2)}, u32[]{:S(2)}) collective-permute-start(bf16[3,1,2,2,256,128]{5,4,3,2,1,0:T(8,128)(2,1)S(1)} %get-tuple-element.7), channel_id=1, source_target_pairs={{2,0},{4,2},{6,4},{8,6},{10,8},{12,10},{14,12},{0,14},{3,1},{5,3},... | collective-permute-start | bytes 2359304 | tf_op jit(solution)/shard_map/ppermute | solution.py:17
  113.1 0.3 fusion.23
  113.4 14.1 %collective-permute-done.12 = bf16[3,1,2,2,256,128]{5,4,3,2,1,0:T(8,128)(2,1)S(1)} collective-permute-done((bf16[3,1,2,2,256,128]{5,4,3,2,1,0:T(8,128)(2,1)S(1)}, bf16[3,1,2,2,256,128]{5,4,3,2,1,0:T(8,128)(2,1)S(1)}, u32[]{:S(2)}, u32[]{:S(2)}) %collective-permute-start.12) | collective-permute-done | bytes 786464 | tf_op jit(solution)/shard_map/ppermute | solution.py:14
  127.5 13.9 %collective-permute-done.11 = bf16[3,1,2,2,256,128]{5,4,3,2,1,0:T(8,128)(2,1)S(1)} collective-permute-done((bf16[3,1,2,2,256,128]{5,4,3,2,1,0:T(8,128)(2,1)S(1)}, bf16[3,1,2,2,256,128]{5,4,3,2,1,0:T(8,128)(2,1)S(1)}, u32[]{:S(2)}, u32[]{:S(2)}) %collective-permute-start.11) | collective-permute-done | bytes 786464 | tf_op jit(solution)/shard_map/ppermute | solution.py:17
  141.4 0.4 pad_maximum_fusion.1
  142.0 3.8 %collective-permute-start.14 = (bf16[3,4,1,2,256,128]{5,4,3,2,1,0:T(8,128)(2,1)S(1)}, bf16[3,4,1,2,256,128]{5,4,3,2,1,0:T(8,128)(2,1)S(1)}, u32[]{:S(2)}, u32[]{:S(2)}) collective-permute-start(bf16[3,4,1,2,256,128]{5,4,3,2,1,0:T(8,128)(2,1)S(1)} %get-tuple-element.2), channel_id=1, source_target_pairs={{0,1},{1,0},{2,3},{3,2},{4,5},{5,4},{6,7},{7,6},{8,9},{9,8},{10,11... | collective-permute-start | bytes 4718600 | tf_op jit(solution)/shard_map/ppermute | solution.py:14
  145.8 1.9 %collective-permute-start.13 = (bf16[3,4,1,2,256,128]{5,4,3,2,1,0:T(8,128)(2,1)S(1)}, bf16[3,4,1,2,256,128]{5,4,3,2,1,0:T(8,128)(2,1)S(1)}, u32[]{:S(2)}, u32[]{:S(2)}) collective-permute-start(bf16[3,4,1,2,256,128]{5,4,3,2,1,0:T(8,128)(2,1)S(1)} %get-tuple-element.3), channel_id=1, source_target_pairs={{1,0},{0,1},{3,2},{2,3},{5,4},{4,5},{7,6},{6,7},{9,8},{8,9},{11,10... | collective-permute-start | bytes 4718600 | tf_op jit(solution)/shard_map/ppermute | solution.py:17
  147.9 0.3 fusion.54
  148.2 0.3 fusion.60
  148.5 0.3 fusion.20
  148.8 0.3 convolution_add_fusion.1
  149.2 0.3 fusion.21
  149.5 0.3 fusion.22
  149.8 1.4 collective-permute-done.13
  151.2 0.3 fusion.32
  151.5 0.7 fusion.14
  152.4 0.3 fusion.24
  152.9 20.5 %all_to_all.5 = bf16[16,1,1,256,128]{4,3,2,1,0:T(8,128)(2,1)S(1)} all-to-all(bf16[16,1,1,256,128]{4,3,2,1,0:T(8,128)(2,1)S(1)} %stack.3), channel_id=1, replica_groups=mesh['ta'=32,'gz'=8,'gy'=2] {'gz','gy'}, dimensions={0} | all-to-all | bytes 2097152 | tf_op jit(solution)/shard_map/all_to_all | solution.py:79
  173.5 1.0 copy.19
  (35 shorter events, 1.9 us)
Async XLA Ops:
  0.6 81.2 %copy-start = (bf16[1,2,2,2,128,128]{5,4,3,2,1,0:T(8,128)(2,1)S(1)}, bf16[1,2,2,2,128,128]{5,4,3,2,1,0:T(8,128)(2,1)}, u32[]{:S(2)}) copy-start(bf16[1,2,2,2,128,128]{5,4,3,2,1,0:T(8,128)(2,1)} %param.6) | copy-start | bytes 786436
  0.6 26.4 %collective-permute-start.1 = (bf16[1,2,2,2,256,128]{5,4,3,2,1,0:T(8,128)(2,1)}, bf16[1,2,2,2,256,128]{5,4,3,2,1,0:T(8,128)(2,1)S(1)}, u32[]{:S(2)}, u32[]{:S(2)}) collective-permute-start(bf16[1,2,2,2,256,128]{5,4,3,2,1,0:T(8,128)(2,1)} %param.5), channel_id=1, source_target_pairs={{0,16},{16,32},{32,48},{48,64},{64,80},{80,96},{96,112},{112,128},... | collective-permute-start | bytes 1572872 | tf_op jit(solution)/shard_map/ppermute | solution.py:14
  5.1 23.0 %collective-permute-start = (bf16[1,2,2,2,256,128]{5,4,3,2,1,0:T(8,128)(2,1)}, bf16[1,2,2,2,256,128]{5,4,3,2,1,0:T(8,128)(2,1)S(1)}, u32[]{:S(2)}, u32[]{:S(2)}) collective-permute-start(bf16[1,2,2,2,256,128]{5,4,3,2,1,0:T(8,128)(2,1)} %param.5), channel_id=1, source_target_pairs={{16,0},{32,16},{48,32},{64,48},{80,64},{96,80},{112,96},{128,112},... | collective-permute-start | bytes 1572872 | tf_op jit(solution)/shard_map/ppermute | solution.py:17
  28.3 6.9 %copy-start.3 = (bf16[4,1,2,2,2,128,128]{6,5,4,3,2,1,0:T(8,128)(2,1)S(1)}, bf16[4,1,2,2,2,128,128]{6,5,4,3,2,1,0:T(8,128)(2,1)}, u32[]{:S(2)}) copy-start(bf16[4,1,2,2,2,128,128]{6,5,4,3,2,1,0:T(8,128)(2,1)} %param.8) | copy-start | bytes 3145732
  28.4 14.5 %copy-start.1 = (bf16[1,2,2,2,256,128]{5,4,3,2,1,0:T(8,128)(2,1)S(1)}, bf16[1,2,2,2,256,128]{5,4,3,2,1,0:T(8,128)(2,1)}, u32[]{:S(2)}) copy-start(bf16[1,2,2,2,256,128]{5,4,3,2,1,0:T(8,128)(2,1)} %param.5) | copy-start | bytes 1572868
  28.4 25.9 %collective-permute-start.2 = (bf16[3,1,2,2,256,128]{5,4,3,2,1,0:T(8,128)(2,1)S(1)}, bf16[3,1,2,2,256,128]{5,4,3,2,1,0:T(8,128)(2,1)S(1)}, u32[]{:S(2)}, u32[]{:S(2)}) collective-permute-start(bf16[3,1,2,2,256,128]{5,4,3,2,1,0:T(8,128)(2,1)S(1)} %get-tuple-element.9), channel_id=1, source_target_pairs={{2,0},{4,2},{6,4},{8,6},{10,8},{12,10},{14,12},{0,14},{3,1},{5,3},... | collective-permute-start | bytes 2359304 | tf_op jit(solution)/shard_map/ppermute | solution.py:17
  33.2 39.9 %collective-permute-start.3 = (bf16[3,1,2,2,256,128]{5,4,3,2,1,0:T(8,128)(2,1)S(1)}, bf16[3,1,2,2,256,128]{5,4,3,2,1,0:T(8,128)(2,1)S(1)}, u32[]{:S(2)}, u32[]{:S(2)}) collective-permute-start(bf16[3,1,2,2,256,128]{5,4,3,2,1,0:T(8,128)(2,1)S(1)} %get-tuple-element.8), channel_id=1, source_target_pairs={{0,2},{2,4},{4,6},{6,8},{8,10},{10,12},{12,14},{14,0},{1,3},{3,5},... | collective-permute-start | bytes 2359304 | tf_op jit(solution)/shard_map/ppermute | solution.py:14
  35.3 47.8 %collective-permute-start.8 = (bf16[1,2,1,2,128,128]{5,4,3,2,1,0:T(8,128)(2,1)S(1)}, bf16[1,2,1,2,128,128]{5,4,3,2,1,0:T(8,128)(2,1)S(1)}, u32[]{:S(2)}, u32[]{:S(2)}) collective-permute-start(bf16[1,2,1,2,128,128]{5,4,3,2,1,0:T(8,128)(2,1)S(1)} %get-tuple-element.23), channel_id=1, source_target_pairs={{1,0},{0,1},{3,2},{2,3},{5,4},{4,5},{7,6},{6,7},{9,8},{8,9},{11,10... | collective-permute-start | bytes 393224 | tf_op jit(solution)/shard_map/ppermute | solution.py:25
  38.9 43.9 %collective-permute-start.6 = (bf16[1,1,2,2,128,128]{5,4,3,2,1,0:T(8,128)(2,1)S(1)}, bf16[1,1,2,2,128,128]{5,4,3,2,1,0:T(8,128)(2,1)S(1)}, u32[]{:S(2)}, u32[]{:S(2)}) collective-permute-start(bf16[1,1,2,2,128,128]{5,4,3,2,1,0:T(8,128)(2,1)S(1)} %get-tuple-element.21), channel_id=1, source_target_pairs={{14,0},{0,2},{2,4},{4,6},{6,8},{8,10},{10,12},{12,14},{15,1},{1,3}... | collective-permute-start | bytes 393224 | tf_op jit(solution)/shard_map/ppermute | solution.py:25
  41.0 41.5 %collective-permute-start.5 = (bf16[1,2,2,2,128,128]{5,4,3,2,1,0:T(8,128)(2,1)S(1)}, bf16[1,2,2,2,128,128]{5,4,3,2,1,0:T(8,128)(2,1)S(1)}, u32[]{:S(2)}, u32[]{:S(2)}) collective-permute-start(bf16[1,2,2,2,128,128]{5,4,3,2,1,0:T(8,128)(2,1)S(1)} %get-tuple-element.10), channel_id=1, source_target_pairs={{496,0},{0,16},{16,32},{32,48},{48,64},{64,80},{80,96},{96,112},{1... | collective-permute-start | bytes 786440 | tf_op jit(solution)/shard_map/ppermute | solution.py:25
  73.7 9.3 %collective-permute-start.7 = (bf16[3,4,1,2,256,128]{5,4,3,2,1,0:T(8,128)(2,1)S(1)}, bf16[3,4,1,2,256,128]{5,4,3,2,1,0:T(8,128)(2,1)S(1)}, u32[]{:S(2)}, u32[]{:S(2)}) collective-permute-start(bf16[3,4,1,2,256,128]{5,4,3,2,1,0:T(8,128)(2,1)S(1)} %get-tuple-element.4), channel_id=1, source_target_pairs={{0,1},{1,0},{2,3},{3,2},{4,5},{5,4},{6,7},{7,6},{8,9},{9,8},{10,11... | collective-permute-start | bytes 4718600 | tf_op jit(solution)/shard_map/ppermute | solution.py:14
  79.3 2.2 %copy-start.2 = (bf16[4,1,2,2,2,128,128]{6,5,4,3,2,1,0:T(8,128)(2,1)S(1)}, bf16[4,1,2,2,2,128,128]{6,5,4,3,2,1,0:T(8,128)(2,1)}, u32[]{:S(2)}) copy-start(bf16[4,1,2,2,2,128,128]{6,5,4,3,2,1,0:T(8,128)(2,1)} %param.7) | copy-start | bytes 3145732
  79.3 5.4 %collective-permute-start.4 = (bf16[3,4,1,2,256,128]{5,4,3,2,1,0:T(8,128)(2,1)S(1)}, bf16[3,4,1,2,256,128]{5,4,3,2,1,0:T(8,128)(2,1)S(1)}, u32[]{:S(2)}, u32[]{:S(2)}) collective-permute-start(bf16[3,4,1,2,256,128]{5,4,3,2,1,0:T(8,128)(2,1)S(1)} %get-tuple-element.5), channel_id=1, source_target_pairs={{1,0},{0,1},{3,2},{2,3},{5,4},{4,5},{7,6},{6,7},{9,8},{8,9},{11,10... | collective-permute-start | bytes 4718600 | tf_op jit(solution)/shard_map/ppermute | solution.py:17
  85.7 18.8 %collective-permute-start.10 = (bf16[1,2,2,2,256,128]{5,4,3,2,1,0:T(8,128)(2,1)S(1)}, bf16[1,2,2,2,256,128]{5,4,3,2,1,0:T(8,128)(2,1)S(1)}, u32[]{:S(2)}, u32[]{:S(2)}) collective-permute-start(bf16[1,2,2,2,256,128]{5,4,3,2,1,0:T(8,128)(2,1)S(1)} %fusion.15), channel_id=1, source_target_pairs={{0,16},{16,32},{32,48},{48,64},{64,80},{80,96},{96,112},{112,128},... | collective-permute-start | bytes 1572872 | tf_op jit(solution)/shard_map/ppermute | solution.py:14
  87.6 17.8 %collective-permute-start.9 = (bf16[1,2,2,2,256,128]{5,4,3,2,1,0:T(8,128)(2,1)S(1)}, bf16[1,2,2,2,256,128]{5,4,3,2,1,0:T(8,128)(2,1)S(1)}, u32[]{:S(2)}, u32[]{:S(2)}) collective-permute-start(bf16[1,2,2,2,256,128]{5,4,3,2,1,0:T(8,128)(2,1)S(1)} %fusion.15), channel_id=1, source_target_pairs={{16,0},{32,16},{48,32},{64,48},{80,64},{96,80},{112,96},{128,112},... | collective-permute-start | bytes 1572872 | tf_op jit(solution)/shard_map/ppermute | solution.py:17
  105.7 21.8 %collective-permute-start.12 = (bf16[3,1,2,2,256,128]{5,4,3,2,1,0:T(8,128)(2,1)S(1)}, bf16[3,1,2,2,256,128]{5,4,3,2,1,0:T(8,128)(2,1)S(1)}, u32[]{:S(2)}, u32[]{:S(2)}) collective-permute-start(bf16[3,1,2,2,256,128]{5,4,3,2,1,0:T(8,128)(2,1)S(1)} %get-tuple-element.6), channel_id=1, source_target_pairs={{0,2},{2,4},{4,6},{6,8},{8,10},{10,12},{12,14},{14,0},{1,3},{3,5},... | collective-permute-start | bytes 2359304 | tf_op jit(solution)/shard_map/ppermute | solution.py:14
  107.9 33.4 %collective-permute-start.11 = (bf16[3,1,2,2,256,128]{5,4,3,2,1,0:T(8,128)(2,1)S(1)}, bf16[3,1,2,2,256,128]{5,4,3,2,1,0:T(8,128)(2,1)S(1)}, u32[]{:S(2)}, u32[]{:S(2)}) collective-permute-start(bf16[3,1,2,2,256,128]{5,4,3,2,1,0:T(8,128)(2,1)S(1)} %get-tuple-element.7), channel_id=1, source_target_pairs={{2,0},{4,2},{6,4},{8,6},{10,8},{12,10},{14,12},{0,14},{3,1},{5,3},... | collective-permute-start | bytes 2359304 | tf_op jit(solution)/shard_map/ppermute | solution.py:17
  142.0 7.4 %collective-permute-start.14 = (bf16[3,4,1,2,256,128]{5,4,3,2,1,0:T(8,128)(2,1)S(1)}, bf16[3,4,1,2,256,128]{5,4,3,2,1,0:T(8,128)(2,1)S(1)}, u32[]{:S(2)}, u32[]{:S(2)}) collective-permute-start(bf16[3,4,1,2,256,128]{5,4,3,2,1,0:T(8,128)(2,1)S(1)} %get-tuple-element.2), channel_id=1, source_target_pairs={{0,1},{1,0},{2,3},{3,2},{4,5},{5,4},{6,7},{7,6},{8,9},{9,8},{10,11... | collective-permute-start | bytes 4718600 | tf_op jit(solution)/shard_map/ppermute | solution.py:14
  145.8 5.3 %collective-permute-start.13 = (bf16[3,4,1,2,256,128]{5,4,3,2,1,0:T(8,128)(2,1)S(1)}, bf16[3,4,1,2,256,128]{5,4,3,2,1,0:T(8,128)(2,1)S(1)}, u32[]{:S(2)}, u32[]{:S(2)}) collective-permute-start(bf16[3,4,1,2,256,128]{5,4,3,2,1,0:T(8,128)(2,1)S(1)} %get-tuple-element.3), channel_id=1, source_target_pairs={{1,0},{0,1},{3,2},{2,3},{5,4},{4,5},{7,6},{6,7},{9,8},{8,9},{11,10... | collective-permute-start | bytes 4718600 | tf_op jit(solution)/shard_map/ppermute | solution.py:17
  151.5 1.0 copy-start.5
  152.4 21.0 %copy-start.4 = (bf16[1,2,2,2,256,128]{5,4,3,2,1,0:T(8,128)(2,1)}, bf16[1,2,2,2,256,128]{5,4,3,2,1,0:T(8,128)(2,1)S(1)}, u32[]{:S(2)}) copy-start(bf16[1,2,2,2,256,128]{5,4,3,2,1,0:T(8,128)(2,1)S(1)} %fusion.14) | copy-start | bytes 1572868
